TPU v7x, 32 devices: a whole 2x2x4 slice. The times are simulated.
32 devices in a mesh: leaf: 8 (over z, x), panel: 4 (over y, core).
Axes of the slice: x: 2, y: 2, z: 4, core: 2. Of those that a mesh axis runs over, the one named last changes fastest.
Arguments:
- upper_rhs: float32 [8, 512, 128], P('leaf'), may hold values from -6 to 6
- upper_panel: float32 [8, 1024, 512], P('leaf', 'panel'), may hold values from -0.25 to 0.25
- upper_inverse: float32 [8, 512, 512], P('leaf'), as said below
- top_index: int32 [8, 1024], P('leaf', 'panel'), may hold values from 0 to 511
- top_solution: float32 [512, 128], P(('leaf', 'panel')), may hold values from -6 to 6
- owner_map: int32 [8], replicated, may hold values from 0 to 7, each once
- parent_list: int32 [256], P(('leaf', 'panel')), may hold values from 0 to 7, as said below
- lower_index: int32 [256, 256], P(('leaf', 'panel')), may hold values from 0 to 511
- lower_panel: float32 [256, 256, 256], P(('leaf', 'panel')), may hold values from -0.5 to 0.5
- lower_rhs: float32 [256, 256, 128], P(('leaf', 'panel')), may hold values from -6 to 6
- lower_inverse: float32 [256, 256, 256], P(('leaf', 'panel')), as said below
Outputs:
- upper_solution: float32 [8, 512, 128], P('leaf', 'panel')
- lower_solution: float32 [256, 256, 128], P(('leaf', 'panel'))
Inputs may be any that keep to these rules, and one draw needn't show every extreme that they name: `owner_map`: each leaf index holds exactly one upper supernode. `parent_list`: the 8 lower supernodes of one device have pairwise different parents. `upper_inverse`: lower triangular with a positive diagonal. `lower_inverse`: lower triangular with a positive diagonal.
All inputs are finite; a program needn't handle non-finite values.
Results may differ from a plain program's by a relative error of at most 0.00007.
Values sent between devices are 32-bit elements; how exact they have to be, the bound alone decides.
No kernel may reach another device: no remote copies, remote signals or barrier semaphores. Data moves between devices by JAX's collectives and lax.ppermute only.
A program may use at most 64 MiB of HBM per device.

v0:
```python
import jax
import jax.numpy as jnp
from jax import lax
from jax.sharding import PartitionSpec as P


def local(
    upper_rhs,
    upper_panel,
    upper_inverse,
    top_index,
    top_solution,
    owner_map,
    parent_list,
    lower_index,
    lower_panel,
    lower_rhs,
    lower_inverse,
):
    highest = lax.Precision.HIGHEST
    panels = lax.axis_size("panel")
    panel_index = lax.axis_index("panel")
    width_upper = upper_rhs.shape[1]
    share = width_upper // panels
    begin = panel_index * share
    top_whole = lax.all_gather(top_solution, ("leaf", "panel"), axis=0, tiled=True)
    gathered = top_whole[top_index[0]]
    panel_rows = upper_panel[0]
    partial_update = jnp.einsum("kw,kr->wr", panel_rows, gathered, precision=highest)
    update = lax.psum(partial_update, "panel")
    reduced = upper_rhs[0] - update
    full_solution = jnp.einsum("kw,kr->wr", upper_inverse[0], reduced, precision=highest)
    own_rows = lax.dynamic_slice_in_dim(full_solution, begin, share, 0)
    position = owner_map[parent_list]
    all_upper = lax.all_gather(full_solution[None], "leaf", axis=0, tiled=True)
    parent_rows = all_upper[position[:, None], lower_index]
    lower_update = jnp.einsum("skw,skr->swr", lower_panel, parent_rows, precision=highest)
    lower_solution = jnp.einsum(
        "skw,skr->swr", lower_inverse, lower_rhs - lower_update, precision=highest
    )
    return (own_rows[None], lower_solution)


def solution(mesh):
    placed = (
        P("leaf", None, None),
        P("leaf", "panel", None),
        P("leaf", None, None),
        P("leaf", "panel"),
        P(("leaf", "panel"), None),
        P(),
        P(("leaf", "panel")),
        P(("leaf", "panel"), None),
        P(("leaf", "panel"), None, None),
        P(("leaf", "panel"), None, None),
        P(("leaf", "panel"), None, None),
    )
    return jax.shard_map(
        local,
        mesh=mesh,
        in_specs=placed,
        out_specs=(P("leaf", "panel", None), P(("leaf", "panel"), None, None)),
        check_vma=False,
    )
```

profile of v0, /device:TPU:0, one launch (start us, length us, event | category | flops | bytes accessed | tf_op | source)
XLA Modules:
  0.0 174.9 jit_solution(9198700522070792228)
XLA Ops:
  7.2 0.0 copy-start
  7.2 0.0 copy-start.3
  7.2 0.0 all-reduce.2.cloned.1.call-start
  7.2 44.3 %all_gather.6 = f32[512,128]{1,0:T(8,128)S(1)} all-gather(f32[16,128]{1,0:T(8,128)} %param.15), channel_id=1, replica_groups=mesh['leaf'=8,'panel'=4] {'leaf','panel'}, dimensions={0}, use_global_device_ids=true | all-gather | bytes 270336 | tf_op jit(solution)/shard_map/all_gather | solution.py:26
  51.5 0.7 compare_select_fusion.1
  52.2 0.0 copy-start.5
  52.2 0.0 copy-start.1
  52.3 0.7 gather_fusion
  53.0 0.0 copy-start.4
  53.0 2.8 %convolution_bitcast_fusion.2 = f32[512,128]{1,0:T(8,128)} fusion(f32[256,128]{1,0:T(8,128)S(1)} %gather_fusion, f32[1,256,512]{2,1,0:T(8,128)} %param.12), kind=kOutput, calls=%fused_computation.6 | convolution fusion | flops 201326592 | bytes 917504 | tf_op jit(solution)/shard_map/kw,kr->wr/dot_general | solution.py:29
  55.8 0.0 all-reduce.2.cloned.1.call-update
  55.8 0.0 all-gather.3.cloned.1.call-start
  55.8 28.2 %all-reduce.2.cloned.1.call-done = f32[512,128]{1,0:T(8,128)} async-done(((f32[512,128]{1,0:T(8,128)}), f32[512,128]{1,0:T(8,128)}) %all-reduce.2.cloned.1.call-update) | async-done | bytes 262160 | tf_op jit(solution)/shard_map/psum | solution.py:30
  84.0 0.0 copy-done.3
  84.0 2.5 %fusion.1 = f32[128,512]{1,0:T(8,128)} fusion(f32[1,512,512]{2,1,0:T(8,128)S(1)} %copy-done.3, f32[512,128]{1,0:T(8,128)} %all-reduce.2.cloned.1.call-done, f32[1,512,128]{2,1,0:T(8,128)} %param.11), kind=kOutput, calls=%fused_computation.7 | convolution fusion | flops 402718720 | bytes 1835008 | tf_op jit(solution)/shard_map/kw,kr->wr/dot_general | solution.py:32
  86.5 0.0 all-gather.3.cloned.1.call-update
  86.6 0.0 copy-done.5
  86.6 0.0 copy-done.1
  86.6 0.6 gather_fusion.1
  87.3 0.0 copy-done.4
  87.3 0.1 fusion.8
  87.3 0.8 dynamic-slice_bitcast_fusion
  88.2 0.7 copy.19
  88.9 47.4 %all-gather.3.cloned.1.call-done = f32[4096,128]{0,1:T(8,128)} async-done(((f32[512,128]{0,1:T(8,128)}), f32[4096,128]{0,1:T(8,128)}) %all-gather.3.cloned.1.call-update) | async-done | bytes 2097168 | tf_op jit(solution)/shard_map/all_gather | solution.py:35
  136.3 2.9 %copy.22 = f32[4096,128]{1,0:T(8,128)} copy(f32[4096,128]{0,1:T(8,128)} %all-gather.3.cloned.1.call-done) | data formatting | bytes 4194304 | tf_op jit(solution)/shard_map/all_gather | solution.py:35
  139.2 20.6 %gather_fusion.2 = f32[2048,128]{1,0:T(8,128)S(1)} fusion(f32[8,512,128]{2,1,0:T(8,128)} %bitcast.43, s32[2048]{0:T(1024)S(1)} %bitcast.42), kind=kCustom, calls=%fused_computation.2 | custom fusion | bytes 2113536 | tf_op jit(solution)/shard_map/gather | solution.py:36
  159.8 0.0 copy-done
  159.8 0.0 copy-start.2
  159.8 4.9 %fusion = f32[8,256,128]{2,1,0:T(8,128)S(1)} fusion(f32[8,256,128]{2,1,0:T(8,128)} %param.20, f32[8,256,128]{2,1,0:T(8,128)S(1)} %bitcast.44, f32[8,256,256]{2,1,0:T(8,128)S(1)} %copy-done), kind=kOutput, calls=%fused_computation.5 | convolution fusion | flops 805568512 | bytes 5242880 | tf_op jit(solution)/shard_map/skw,skr->swr/dot_general | solution.py:37
  164.7 0.0 copy-done.2
  164.7 2.0 %convolution_bitcast_fusion = f32[8,256,128]{1,2,0:T(8,128)S(1)} fusion(f32[8,256,128]{2,1,0:T(8,128)S(1)} %fusion, f32[8,256,256]{2,1,0:T(8,128)S(1)} %copy-done.2), kind=kOutput, calls=%fused_computation.3 | convolution fusion | flops 805306368 | bytes 4194304 | tf_op jit(solution)/shard_map/skw,skr->swr/dot_general | solution.py:38
  166.7 1.3 copy.20
  (5 shorter events, 0.0 us)
Async XLA Ops:
  7.2 152.6 %copy-start = (f32[8,256,256]{2,1,0:T(8,128)S(1)}, f32[8,256,256]{2,1,0:T(8,128)}, u32[]{:S(2)}) copy-start(f32[8,256,256]{2,1,0:T(8,128)} %param.19) | copy-start | bytes 6291460
  7.2 76.8 %copy-start.3 = (f32[1,512,512]{2,1,0:T(8,128)S(1)}, f32[1,512,512]{2,1,0:T(8,128)}, u32[]{:S(2)}) copy-start(f32[1,512,512]{2,1,0:T(8,128)} %param.13) | copy-start | bytes 3145732
  7.2 76.8 %all-reduce.2.cloned.1.call-start = ((), (), s32[]{:S(2)}) async-start(), calls=%async_computation | async-start | bytes 524288 | tf_op jit(solution)/shard_map/psum | solution.py:30
  52.2 34.3 %copy-start.5 = (s32[8]{0:T(128)S(1)}, s32[8]{0:T(128)}, u32[]{:S(2)}) copy-start(s32[8]{0:T(128)} %param.17) | copy-start | bytes 100
  52.2 34.3 %copy-start.1 = (s32[8]{0:T(128)S(1)}, s32[8]{0:T(128)}, u32[]{:S(2)}) copy-start(s32[8]{0:T(128)} %param.16) | copy-start | bytes 100
  53.0 34.3 %copy-start.4 = (s32[8,256]{1,0:T(8,128)S(1)}, s32[8,256]{1,0:T(8,128)}, u32[]{:S(2)}) copy-start(s32[8,256]{1,0:T(8,128)} %param.18) | copy-start | bytes 24580
  55.8 80.5 %all-gather.3.cloned.1.call-start = ((), (), s32[]{:S(2)}) async-start(), calls=%async_computation.1 | async-start | bytes 2359296 | tf_op jit(solution)/shard_map/all_gather | solution.py:35
  159.8 4.9 %copy-start.2 = (f32[8,256,256]{2,1,0:T(8,128)S(1)}, f32[8,256,256]{2,1,0:T(8,128)}, u32[]{:S(2)}) copy-start(f32[8,256,256]{2,1,0:T(8,128)} %param.21) | copy-start | bytes 6291460
Sparse Core Ops, SparseCore 0:
  55.9 28.0 all-reduce.1
  87.0 49.2 all-gather.2
where the time goes:
time: 175 us
  waiting for transfers between devices  75.6 us (43%)
  blocking collectives  44.3 us (25%)
  local copies, waits for them, and re-layouts  27.8 us (16%)
  between operations  14.2 us (8%)
  matrix products  12.2 us (7%)
    all_gather x1, waiting for transfers between devices, local(): all_upper = lax.all_gather(full_solution[None], 'leaf', axis=0, tiled=True)  47.4 us
    all_gather x1, blocking collectives, local(): lax.all_gather(top_solution, ('leaf', 'panel'), axis=0, tiled=True)  44.3 us
    psum x1, waiting for transfers between devices, local(): update = lax.psum(partial_update, 'panel')  28.2 us
    gather x1, local copies, waits for them, and re-layouts, local(): parent_rows = all_upper[position[:, None], lower_index]  20.6 us
    dot_general x1, matrix products, local(): jnp.einsum('skw,skr->swr', lower_panel, parent_rows, precision=highest)  4.89 us
  transfers between devices with their start and end apart: 2, of which 2 were waited for; matrix products, arithmetic and copies ran while one was open for 1% of the time, Pallas kernels for 0%

commit v1 on v0

--- a/solution.py
+++ b/solution.py
@@ -27,7 +27,7 @@
     gathered = top_whole[top_index[0]]
     panel_rows = upper_panel[0]
     partial_update = jnp.einsum("kw,kr->wr", panel_rows, gathered, precision=highest)
-    update = lax.psum(partial_update, "panel")
+    update = jnp.sum(lax.all_gather(partial_update, "panel"), axis=0)
     reduced = upper_rhs[0] - update
     full_solution = jnp.einsum("kw,kr->wr", upper_inverse[0], reduced, precision=highest)
     own_rows = lax.dynamic_slice_in_dim(full_solution, begin, share, 0)

time: 175 us -> 160 us (0.914)
  waiting for transfers between devices: 75.6 us -> 56.7 us
  local copies, waits for them, and re-layouts: 27.8 us -> 33.1 us
  matrix products: 12.2 us -> 9.73 us
    psum x1 -> x0, waiting for transfers between devices: 28.2 us -> none  [local(): update = lax.psum(partial_update, 'panel')]
    all_gather x0 -> x1, waiting for transfers between devices: none -> 12.1 us  [local(): update = jnp.sum(lax.all_gather(partial_update, 'panel'), axis=0)]
    unnamed x15 -> x17, local copies, waits for them, and re-layouts: 2.08 us -> 5.45 us
    all_gather x1, waiting for transfers between devices: 47.4 us -> 44.5 us  [local(): all_upper = lax.all_gather(full_solution[None], 'leaf', axis=0, tiled=True)]
    all_gather x0 -> x1, local copies, waits for them, and re-layouts: none -> 1.93 us  [local(): update = jnp.sum(lax.all_gather(partial_update, 'panel'), axis=0)]
  transfers between devices with their start and end apart: 2 -> 2, of which waited for: 2 -> 2; matrix products, arithmetic and copies ran while one was open for 1% -> 4% of each run, Pallas kernels for 0% -> 0%
where the time goes in v1:
time: 160 us; the launch traced here: 159 us
  waiting for transfers between devices  56.7 us (35%)
  blocking collectives  44.3 us (28%)
  local copies, waits for them, and re-layouts  33.1 us (21%)
  between operations  14.2 us (9%)
  matrix products  9.73 us (6%)
    all_gather x1, waiting for transfers between devices, local(): all_upper = lax.all_gather(full_solution[None], 'leaf', axis=0, tiled=True)  44.5 us
    all_gather x1, blocking collectives, local(): lax.all_gather(top_solution, ('leaf', 'panel'), axis=0, tiled=True)  44.3 us
    gather x1, local copies, waits for them, and re-layouts, local(): parent_rows = all_upper[position[:, None], lower_index]  20.6 us
    all_gather x1, waiting for transfers between devices, local(): update = jnp.sum(lax.all_gather(partial_update, 'panel'), axis=0)  12.1 us
    unnamed x17, local copies, waits for them, and re-layouts  5.45 us
    dot_general x1, matrix products, local(): jnp.einsum('skw,skr->swr', lower_panel, parent_rows, precision=highest)  3.41 us
  transfers between devices with their start and end apart: 2, of which 2 were waited for; matrix products, arithmetic and copies ran while one was open for 4% of the time, Pallas kernels for 0%

profile of v1, /device:TPU:0, one launch (start us, length us, event | category | flops | bytes accessed | tf_op | source)
XLA Modules:
  0.0 159.4 jit_solution(5784519744121307920)
XLA Ops:
  7.2 0.0 copy-start
  7.2 0.0 copy-start.3
  7.2 0.0 all-gather.5.cloned.1.call-start
  7.2 44.3 %all_gather.12 = f32[512,128]{1,0:T(8,128)S(1)} all-gather(f32[16,128]{1,0:T(8,128)} %param.15), channel_id=1, replica_groups=mesh['leaf'=8,'panel'=4] {'leaf','panel'}, dimensions={0}, use_global_device_ids=true | all-gather | bytes 270336 | tf_op jit(solution)/shard_map/all_gather | solution.py:26
  51.5 0.7 compare_select_fusion.1
  52.2 0.7 gather_fusion
  53.0 2.2 %convolution_bitcast_fusion.2 = f32[512,128]{0,1:T(8,128)} fusion(f32[256,128]{1,0:T(8,128)S(1)} %gather_fusion, f32[1,256,512]{2,1,0:T(8,128)} %param.12), kind=kOutput, calls=%fused_computation.6 | convolution fusion | flops 201326592 | bytes 917504 | tf_op jit(solution)/shard_map/kw,kr->wr/dot_general | solution.py:29
  55.2 0.0 all-gather.5.cloned.1.call-update
  55.2 0.0 all-gather.7.cloned.1.call-start
  55.2 0.0 copy-done.3
  55.3 0.8 copy.21
  56.1 12.1 %all-gather.5.cloned.1.call-done = f32[2048,128]{0,1:T(8,128)} async-done(((f32[512,128]{0,1:T(8,128)}), f32[2048,128]{0,1:T(8,128)}) %all-gather.5.cloned.1.call-update) | async-done | bytes 1048592 | tf_op jit(solution)/shard_map/all_gather | solution.py:30
  68.2 1.9 %reshape.67 = f32[4,512,128]{1,0,2:T(4,128)S(1)} reshape(f32[2048,128]{0,1:T(8,128)} %all-gather.5.cloned.1.call-done) | data formatting | bytes 2097152 | tf_op jit(solution)/shard_map/all_gather | solution.py:30
  70.1 0.0 copy-start.5
  70.1 0.0 copy-start.1
  70.2 0.0 copy-start.4
  70.2 0.6 reduce_sum.11
  70.8 2.7 %fusion.1 = f32[128,512]{1,0:T(8,128)} fusion(f32[1,512,512]{2,1,0:T(8,128)} %param.13, f32[1,512,128]{1,2,0:T(8,128)} %copy.21, f32[512,128]{0,1:T(8,128)S(1)} %reduce_sum.11), kind=kOutput, calls=%fused_computation.7 | convolution fusion | flops 402718720 | bytes 1835008 | tf_op jit(solution)/shard_map/kw,kr->wr/dot_general | solution.py:32
  73.5 0.0 all-gather.7.cloned.1.call-update
  73.6 0.0 copy-done.5
  73.6 0.0 copy-done.1
  73.6 0.6 gather_fusion.1
  74.3 0.0 copy-done.4
  74.3 0.1 fusion.9
  74.3 2.5 %copy.24 = f32[8,256,128]{1,2,0:T(8,128)} copy(f32[8,256,128]{2,1,0:T(8,128)} %param.20) | data formatting | bytes 2097152 | tf_op args[9]
  76.9 0.8 dynamic-slice_bitcast_fusion
  77.7 0.7 copy.25
  78.4 44.5 %all-gather.7.cloned.1.call-done = f32[4096,128]{0,1:T(8,128)} async-done(((f32[512,128]{0,1:T(8,128)}), f32[4096,128]{0,1:T(8,128)}) %all-gather.7.cloned.1.call-update) | async-done | bytes 2097168 | tf_op jit(solution)/shard_map/all_gather | solution.py:35
  123.0 2.9 %copy.28 = f32[4096,128]{1,0:T(8,128)} copy(f32[4096,128]{0,1:T(8,128)} %all-gather.7.cloned.1.call-done) | data formatting | bytes 4194304 | tf_op jit(solution)/shard_map/all_gather | solution.py:35
  125.9 20.6 %gather_fusion.2 = f32[2048,128]{1,0:T(8,128)S(1)} fusion(f32[8,512,128]{2,1,0:T(8,128)} %bitcast.50, s32[2048]{0:T(1024)S(1)} %bitcast.49), kind=kCustom, calls=%fused_computation.2 | custom fusion | bytes 2113536 | tf_op jit(solution)/shard_map/gather | solution.py:36
  146.5 0.0 copy-done
  146.5 0.0 copy-start.2
  146.5 3.4 %fusion = f32[8,256,128]{1,2,0:T(8,128)S(1)} fusion(f32[8,256,128]{1,2,0:T(8,128)} %copy.24, f32[8,256,128]{2,1,0:T(8,128)S(1)} %bitcast.51, f32[8,256,256]{2,1,0:T(8,128)S(1)} %copy-done), kind=kOutput, calls=%fused_computation.5 | convolution fusion | flops 805568512 | bytes 5242880 | tf_op jit(solution)/shard_map/skw,skr->swr/dot_general | solution.py:37
  149.9 0.0 copy-done.2
  149.9 1.4 convolution_bitcast_fusion
  151.3 1.3 copy.26
  (5 shorter events, 0.0 us)
Async XLA Ops:
  7.2 139.3 %copy-start = (f32[8,256,256]{2,1,0:T(8,128)S(1)}, f32[8,256,256]{2,1,0:T(8,128)}, u32[]{:S(2)}) copy-start(f32[8,256,256]{2,1,0:T(8,128)} %param.19) | copy-start | bytes 6291460
  7.2 48.1 %copy-start.3 = (f32[1,512,128]{2,1,0:T(8,128)S(1)}, f32[1,512,128]{2,1,0:T(8,128)}, u32[]{:S(2)}) copy-start(f32[1,512,128]{2,1,0:T(8,128)} %param.11) | copy-start | bytes 786436
  7.2 61.0 %all-gather.5.cloned.1.call-start = ((), (), s32[]{:S(2)}) async-start(), calls=%async_computation | async-start | bytes 1310720 | tf_op jit(solution)/shard_map/all_gather | solution.py:30
  55.2 67.8 %all-gather.7.cloned.1.call-start = ((), (), s32[]{:S(2)}) async-start(), calls=%async_computation.1 | async-start | bytes 2359296 | tf_op jit(solution)/shard_map/all_gather | solution.py:35
  70.1 3.4 %copy-start.5 = (s32[8]{0:T(128)S(1)}, s32[8]{0:T(128)}, u32[]{:S(2)}) copy-start(s32[8]{0:T(128)} %param.17) | copy-start | bytes 100
  70.1 3.5 %copy-start.1 = (s32[8]{0:T(128)S(1)}, s32[8]{0:T(128)}, u32[]{:S(2)}) copy-start(s32[8]{0:T(128)} %param.16) | copy-start | bytes 100
  70.2 4.1 %copy-start.4 = (s32[8,256]{1,0:T(8,128)S(1)}, s32[8,256]{1,0:T(8,128)}, u32[]{:S(2)}) copy-start(s32[8,256]{1,0:T(8,128)} %param.18) | copy-start | bytes 24580
  146.5 3.4 %copy-start.2 = (f32[8,256,256]{2,1,0:T(8,128)S(1)}, f32[8,256,256]{2,1,0:T(8,128)}, u32[]{:S(2)}) copy-start(f32[8,256,256]{2,1,0:T(8,128)} %param.21) | copy-start | bytes 6291460
Sparse Core Ops, SparseCore 0:
  55.3 12.8 all-gather.4
  73.7 49.2 all-gather.6
